TPU v7x, 256 devices: a whole 4x4x8 slice. The times are simulated.
256 devices in a mesh: gx: 16 (over x, y), gy: 16 (over z, core).
Axes of the slice: x: 4, y: 4, z: 8, core: 2. Of those that a mesh axis runs over, the one named last changes fastest.
Arguments:
- tokens: bfloat16 [2048, 2048], P('gy', 'gx'), may hold values from -6 to 6
- gain: bfloat16 [2048], P('gx'), may hold values from 0.5 to 1.5
- w_router: bfloat16 [2048, 8], P('gx'), may hold values from -0.25 to 0.25
- expert_query_weight: bfloat16 [8, 2048, 16, 128], P(None, 'gx', 'gy'), may hold values from -0.25 to 0.25
- key_value_weight: bfloat16 [2048, 16, 256], P('gx', 'gy'), may hold values from -0.125 to 0.125
- expert_output_weight: bfloat16 [8, 16, 128, 2048], P(None, 'gy', None, 'gx'), may hold values from -0.25 to 0.25
- cache_keys: bfloat16 [16, 16, 4096, 128], P('gx', 'gy'), may hold values from -1220 to 1220
- cached_value_slots: bfloat16 [16, 16, 4096, 128], P('gx', 'gy'), may hold values from -6 to 6
- lengths: int32 [16], replicated, may hold values from 1 to 4096, 34816 in all
- deal: int32 [16], replicated, may hold values from 0 to 15, each once
- route: int32 [2048, 2], replicated, may hold values from 0 to 7, all different within a row
Outputs:
- mixed: bfloat16 [2048, 2048], P('gy', 'gx')
Inputs may be any that keep to these rules, and one draw needn't show every extreme that they name: `lengths`: each request's cache holds between 1 and 4096 keys, and the longest holds exactly 4096. deal[r] is the cache slot of request r; every slot is used once. `route`: each token names 2 different attention experts.
All inputs are finite; a program needn't handle non-finite values.
Results may differ from a plain program's by a relative error of at most 0.01.
The roundings to bfloat16 on the way count: a program that leaves them out, or rounds other values in their place, can miss the bound.
Values may be sent and summed in bfloat16 or wider, within the bound.
No kernel may reach another device: no remote copies, remote signals or barrier semaphores. Data moves between devices by JAX's collectives and lax.ppermute only.
A program may use at most 64 MiB of HBM per device.

v0:
```python
import jax
import jax.numpy as jnp
from jax import lax
from jax.sharding import PartitionSpec as P

masked_score = -1e30
norm_eps = 1e-06


def expert_onehot(route_rows, experts):
    return (route_rows[:, :, None] == jnp.arange(experts, dtype=jnp.int32)[None, None, :]).astype(
        jnp.float32
    )


def absorb(carry_state, scores, value_rows):
    running_max, running_sum, accumulated = carry_state
    new_max = jnp.maximum(running_max, jnp.max(scores, axis=2))
    shrink = jnp.exp(running_max - new_max)
    weights = jnp.exp(scores - new_max[:, :, None])
    running_sum = running_sum * shrink + jnp.sum(weights, axis=2)
    accumulated = accumulated * shrink[:, :, None] + jnp.einsum(
        "hrk,hkd->hrd", weights.astype(jnp.bfloat16), value_rows, preferred_element_type=jnp.float32
    )
    return (new_max, running_sum, accumulated)


def per_device(
    tokens,
    gain,
    w_router,
    expert_query_weight,
    key_value_weight,
    expert_output_weight,
    cache_keys,
    cached_value_slots,
    lengths,
    deal,
    route,
):
    requests = lengths.shape[0]
    experts = expert_query_weight.shape[0]
    heads_local = expert_query_weight.shape[2]
    head_dim = expert_query_weight.shape[3]
    top_count = route.shape[1]
    gathered = lax.all_gather(tokens, "gy", axis=0, tiled=True)
    total_rows, local_width = gathered.shape
    new_len = total_rows // requests
    full_width = local_width * lax.axis_size("gx")
    slot_index = lax.axis_index("gx")
    inverse = jnp.zeros((requests,), jnp.int32).at[deal].set(jnp.arange(requests, dtype=jnp.int32))
    ordered = jnp.take(gathered.reshape(requests, new_len, local_width), inverse, axis=0).reshape(
        total_rows, local_width
    )
    slot_route = jnp.take(route.reshape(requests, new_len, top_count), inverse, axis=0).reshape(
        total_rows, top_count
    )
    widened = ordered.astype(jnp.float32)
    squares = jnp.sum(widened * widened, axis=1)
    scaled_input = (widened * gain.astype(jnp.float32)[None, :]).astype(jnp.bfloat16)
    router_part = jnp.dot(scaled_input, w_router, preferred_element_type=jnp.float32)
    query_part = jnp.einsum(
        "td,edhk->tehk", scaled_input, expert_query_weight, preferred_element_type=jnp.float32
    )
    keyval_part = jnp.einsum(
        "td,dhk->thk", scaled_input, key_value_weight, preferred_element_type=jnp.float32
    )
    my_route = lax.dynamic_slice_in_dim(slot_route, slot_index * new_len, new_len, 0)
    my_onehot = expert_onehot(my_route, experts)
    query_all, keyval_sums, router_sums, square_sums = (
        lax.psum_scatter(query_part, "gx", scatter_dimension=0, tiled=True),
        lax.psum_scatter(keyval_part, "gx", scatter_dimension=0, tiled=True),
        lax.psum_scatter(router_part, "gx", scatter_dimension=0, tiled=True),
        lax.psum_scatter(squares, "gx", scatter_dimension=0, tiled=True),
    )
    query_totals = jnp.sum(my_onehot[:, :, :, None, None] * query_all[:, None], axis=2)
    inverse_root_mean = lax.rsqrt(square_sums / full_width + norm_eps)
    logits = router_sums * inverse_root_mean[:, None]
    chosen = jnp.sum(my_onehot * logits[:, None, :], axis=2)
    gate_gap = chosen[:, 0] - chosen[:, 1]
    gate_weights = jnp.stack([jax.nn.sigmoid(gate_gap), jax.nn.sigmoid(-gate_gap)], axis=1).astype(
        jnp.bfloat16
    )
    query_matrix = (query_totals * inverse_root_mean[:, None, None, None]).astype(jnp.bfloat16)
    key_value_rows = (keyval_sums * inverse_root_mean[:, None, None]).astype(jnp.bfloat16)
    query_rows = new_len * top_count
    query_by_head = jnp.transpose(query_matrix, (2, 0, 1, 3)).reshape(
        heads_local, query_rows, head_dim
    )
    fresh_keyval = jnp.transpose(key_value_rows, (1, 0, 2))
    fresh_keys = fresh_keyval[:, :, :head_dim]
    fresh_values = fresh_keyval[:, :, head_dim:]
    length = jnp.take(lengths, jnp.take(inverse, slot_index))
    local_keys = cache_keys[0]
    local_values = cached_value_slots[0]
    cache_span = local_keys.shape[1]
    key_block = min(1024, cache_span)
    score_scale = head_dim ** (-0.5)
    initial = (
        jnp.full((heads_local, query_rows), masked_score, jnp.float32),
        jnp.zeros((heads_local, query_rows), jnp.float32),
        jnp.zeros((heads_local, query_rows, head_dim), jnp.float32),
    )

    def visit_block(block_index, carry_state):
        first_key = block_index * key_block
        key_rows = lax.dynamic_slice_in_dim(local_keys, first_key, key_block, 1)
        value_rows = lax.dynamic_slice_in_dim(local_values, first_key, key_block, 1)
        scores = (
            jnp.einsum("hrd,hkd->hrk", query_by_head, key_rows, preferred_element_type=jnp.float32)
            * score_scale
        )
        visible = first_key + jnp.arange(key_block, dtype=jnp.int32) < length
        scores = jnp.where(visible[None, None, :], scores, masked_score)
        return absorb(carry_state, scores, value_rows)

    block_count = (length + key_block - 1) // key_block
    carry_state = lax.fori_loop(0, block_count, visit_block, initial)
    fresh_scores = (
        jnp.einsum("hrd,hkd->hrk", query_by_head, fresh_keys, preferred_element_type=jnp.float32)
        * score_scale
    )
    causal = (
        jnp.arange(new_len, dtype=jnp.int32)[None, :]
        <= (jnp.arange(query_rows, dtype=jnp.int32) // top_count)[:, None]
    )
    fresh_scores = jnp.where(causal[None], fresh_scores, masked_score)
    running_max, running_sum, accumulated = absorb(carry_state, fresh_scores, fresh_values)
    attended_output = (accumulated / running_sum[:, :, None]).astype(jnp.bfloat16)
    attended_output = jnp.transpose(
        attended_output.reshape(heads_local, new_len, top_count, head_dim), (1, 2, 0, 3)
    ).reshape(new_len, top_count * heads_local * head_dim)
    all_attended, all_gates = (
        lax.all_gather(attended_output, "gx", axis=0, tiled=True),
        lax.all_gather(gate_weights, "gx", axis=0, tiled=True),
    )
    token_attended = jnp.take(
        all_attended.reshape(requests, new_len, top_count * heads_local * head_dim), deal, axis=0
    ).reshape(total_rows, top_count, heads_local, head_dim)
    token_gates = (
        jnp.take(all_gates.reshape(requests, new_len, top_count), deal, axis=0)
        .reshape(total_rows, top_count)
        .astype(jnp.float32)
    )
    wide_output = expert_output_weight.astype(jnp.float32)
    piece = token_attended.astype(jnp.float32)
    mixing = expert_onehot(route, experts) * token_gates[:, :, None]
    folded = jnp.einsum("tse,tshd->tehd", mixing, piece, precision=lax.Precision.HIGHEST)
    output_sum = lax.psum_scatter(
        jnp.einsum("tehd,ehdo->to", folded, wide_output, precision=lax.Precision.HIGHEST),
        "gy",
        scatter_dimension=0,
        tiled=True,
    )
    return output_sum.astype(jnp.bfloat16)


def solution(mesh):
    placed = (
        P("gy", "gx"),
        P("gx"),
        P("gx", None),
        P(None, "gx", "gy", None),
        P("gx", "gy", None),
        P(None, "gy", None, "gx"),
        P("gx", "gy", None, None),
        P("gx", "gy", None, None),
        P(),
        P(),
        P(),
    )
    return jax.shard_map(
        per_device, mesh=mesh, in_specs=placed, out_specs=P("gy", "gx"), check_vma=False
    )
```

profile of v0, /device:TPU:8, one launch (start us, length us, event | category | flops | bytes accessed | tf_op | source)
XLA Modules:
  0.0 427.1 jit_solution(1710121038791396708)
XLA Ops:
  6.5 0.0 copy-start
  6.5 0.7 compare_select_fusion.3
  7.2 0.6 scatter_custom_fusion
  7.9 0.7 convert_element_type.98
  8.6 21.6 %all_gather.9 = bf16[2048,128]{1,0:T(8,128)(2,1)S(1)} all-gather(bf16[128,128]{1,0:T(8,128)(2,1)} %param.13), channel_id=1, replica_groups=mesh['gx'=16,'gy'=16] {'gy'}, dimensions={0}, use_global_device_ids=true | all-gather | bytes 557056 | tf_op jit(solution)/shard_map/all_gather | solution.py:46
  30.2 0.6 gather_fusion.1
  30.9 0.4 fusion.24
  31.3 2.6 convolution_bitcast_fusion.2
  33.9 0.0 reduce-scatter.9.cloned.1.call-update
  34.0 0.0 reduce-scatter.7.cloned.1.call-start
  34.0 0.0 copy-start.3
  34.0 0.0 copy-start.4
  34.0 0.0 copy-start.1
  34.1 4.5 %convolution_bitcast_fusion.1 = f32[2048,8,1,128]{3,0,1,2:T(8,128)} fusion(bf16[2048,128,1]{1,0,2:T(8,128)(2,1)S(1)} %bitcast.115, bf16[8,128,1,128]{3,1,2,0:T(8,128)(2,1)S(1)} %copy-done), kind=kOutput, calls=%fused_computation.25 | convolution fusion | flops 536870912 | bytes 9175040 | tf_op jit(solution)/shard_map/td,edhk->tehk/dot_general | solution.py:62
  38.5 0.0 reduce-scatter.7.cloned.1.call-update
  38.5 0.0 reduce-scatter.5.cloned.1.call-start
  38.6 0.1 broadcast_bitcast_fusion
  38.7 0.3 bitcast_select_fusion
  39.0 0.9 fusion.29
  39.9 0.0 reduce-scatter.5.cloned.1.call-update
  39.9 0.0 all-gather.2.cloned.1.call-start
  40.0 0.6 dynamic-slice.4
  41.2 0.6 dynamic-slice.5
  42.5 0.1 dynamic-slice.8
  42.6 0.6 gather_fusion
  43.2 0.1 copy.43
  43.3 37.2 %all-reduce = f32[2048]{0:T(1024)S(1)} all-reduce(f32[2048]{0:T(1024)S(1)} %bitcast.128), channel_id=3, replica_groups=mesh['gx'=16,'gy'=16] {'gx'}, use_global_device_ids=true, to_apply=%region_3.4.clone | all-reduce | flops 2048 | bytes 16384
  80.6 0.0 copy-done.6
  80.6 0.6 dynamic-slice.6
  81.8 0.1 fusion.44
  81.9 0.1 mul.177
  82.0 0.2 mul.178
  82.1 30.0 %reduce-scatter.9.cloned.1.call-done = f32[128,1,256]{2,0,1:T(8,128)} async-done(((f32[2048,1,256]{2,0,1:T(8,128)}), f32[128,1,256]{2,0,1:T(8,128)}) %reduce-scatter.9.cloned.1.call-update) | async-done | bytes 131088 | tf_op jit(solution)/shard_map/reduce_scatter | solution.py:72
  112.1 1.0 fusion.38
  113.1 92.9 %reduce-scatter.7.cloned.1.call-done = f32[128,8,1,128]{3,0,1,2:T(8,128)} async-done(((f32[2048,8,1,128]{3,0,1,2:T(8,128)}), f32[128,8,1,128]{3,0,1,2:T(8,128)}) %reduce-scatter.7.cloned.1.call-update) | async-done | bytes 524304 | tf_op jit(solution)/shard_map/reduce_scatter | solution.py:71
  206.1 1.3 copy.44
  207.4 0.4 multiply_reduce_fusion
  207.9 0.2 multiply_convert_fusion.3
  208.1 0.1 fusion.34
  208.2 0.0 copy-start.5
  208.2 3.0 while.16
  208.3 1.3 fusion.62
  209.6 0.2 fusion.63
  209.8 1.3 fusion.64
  211.2 0.2 fusion.50
  211.5 0.2 fusion.23
  211.7 0.6 reshape_transpose_reshape.3
  212.3 0.0 all-gather.2.cloned.1.call-update
  212.3 0.0 reduce-scatter.11.cloned.1.call-start
  212.4 0.4 copy.41
  212.8 0.1 broadcast_bitcast_fusion.1
  212.9 72.9 %reduce-scatter.5.cloned.1.call-done = f32[128,8]{0,1:T(8,128)} async-done(((f32[2048,8]{0,1:T(8,128)}), f32[128,8]{0,1:T(8,128)}) %reduce-scatter.5.cloned.1.call-update) | async-done | bytes 4112 | tf_op jit(solution)/shard_map/reduce_scatter | solution.py:73
  285.8 0.7 broadcast_multiply_fusion
  286.6 19.8 %all_gather.10 = bf16[2048,2]{0,1:T(2,128)(2,1)S(1)} all-gather(bf16[128,2]{0,1:T(2,128)(2,1)S(1)} %pad_maximum_fusion), channel_id=1, replica_groups=mesh['gx'=16,'gy'=16] {'gx'}, dimensions={0}, use_global_device_ids=true | all-gather | bytes 8704 | tf_op jit(solution)/shard_map/all_gather | solution.py:135
  306.4 0.6 gather_fusion.2
  307.0 0.4 copy.42
  307.4 27.6 %all-gather.2.cloned.1.call-done = bf16[2048,256]{1,0:T(8,128)(2,1)} async-done(((bf16[128,256]{1,0:T(8,128)(2,1)}), bf16[2048,256]{1,0:T(8,128)(2,1)}) %all-gather.2.cloned.1.call-update) | async-done | bytes 1048592 | tf_op jit(solution)/shard_map/all_gather | solution.py:134
  335.0 1.8 gather_fusion.3
  336.8 1.1 gather.40
  337.9 17.2 %fusion.18 = f32[2048,8,128]{2,1,0:T(8,128)S(1)} fusion(bf16[2048,2,128]{2,1,0:T(2,128)(2,1)} %gather.40, pred[2048]{0:T(1024)(128)(4,1)S(1)} %broadcast_bitcast_fusion.1, f32[2048,2]{1,0:T(8,128)S(1)} %copy.42, s32[2048,2]{1,0:T(8,128)S(1)} %copy.41), kind=kOutput, calls=%fused_computation.29 | convolution fusion | flops 50921472 | bytes 9472000 | tf_op jit(solution)/shard_map/tse,tshd->tehd/dot_general | solution.py:148
  355.2 5.6 %fusion.15 = f32[2048,128]{1,0:T(8,128)} fusion(f32[2048,8,128]{2,1,0:T(8,128)S(1)} %fusion.18, bf16[8,1,128,128]{3,2,1,0:T(8,128)(2,1)S(1)} %copy-done.2), kind=kOutput, calls=%fused_computation.28 | convolution fusion | flops 3221225472 | bytes 9699328 | tf_op jit(solution)/shard_map/tehd,ehdo->to/dot_general | solution.py:150
  360.8 0.0 reduce-scatter.11.cloned.1.call-update
  360.9 58.2 %reduce-scatter.11.cloned.1.call-done = f32[128,128]{1,0:T(8,128)} async-done(((f32[2048,128]{1,0:T(8,128)}), f32[128,128]{1,0:T(8,128)}) %reduce-scatter.11.cloned.1.call-update) | async-done | bytes 65552 | tf_op jit(solution)/shard_map/reduce_scatter | solution.py:149
  419.1 1.5 convert_element_type.111
  (32 shorter events, 0.2 us)
Async XLA Ops:
  6.5 27.5 %copy-start = (bf16[8,128,1,128]{3,1,2,0:T(8,128)(2,1)S(1)}, bf16[8,128,1,128]{3,1,2,0:T(8,128)(2,1)}, u32[]{:S(2)}) copy-start(bf16[8,128,1,128]{3,1,2,0:T(8,128)(2,1)} %param.16) | copy-start | bytes 786436
  6.5 105.6 %reduce-scatter.9.cloned.1.call-start = ((), (), s32[]{:S(2)}) async-start(), calls=%async_computation.6 | async-start | bytes 2228224 | tf_op jit(solution)/shard_map/reduce_scatter | solution.py:72
  34.0 172.1 %reduce-scatter.7.cloned.1.call-start = ((), (), s32[]{:S(2)}) async-start(), calls=%async_computation.5 | async-start | bytes 8912896 | tf_op jit(solution)/shard_map/reduce_scatter | solution.py:71
  34.0 5.0 %copy-start.3 = (bf16[128,8]{0,1:T(8,128)(2,1)S(1)}, bf16[128,8]{0,1:T(8,128)(2,1)}, u32[]{:S(2)}) copy-start(bf16[128,8]{0,1:T(8,128)(2,1)} %param.15) | copy-start | bytes 6148
  34.0 7.2 %copy-start.4 = (s32[16]{0:T(128)S(1)}, s32[16]{0:T(128)}, u32[]{:S(2)}) copy-start(s32[16]{0:T(128)} %param.21) | copy-start | bytes 196
  34.0 8.5 %copy-start.1 = (s32[2048,2]{0,1:T(2,128)S(1)}, s32[2048,2]{0,1:T(2,128)}, u32[]{:S(2)}) copy-start(s32[2048,2]{0,1:T(2,128)} %param.23) | copy-start | bytes 49156
  38.5 42.1 %copy-start.6 = (u32[256]{0:T(256)S(1)}, u32[256]{0:T(256)}, u32[]{:S(2)}) copy-start(u32[256]{0:T(256)} %constant.201) | copy-start | bytes 3076
  38.5 247.3 %reduce-scatter.5.cloned.1.call-start = ((), (), s32[]{:S(2)}) async-start(), calls=%async_computation.4 | async-start | bytes 69632 | tf_op jit(solution)/shard_map/reduce_scatter | solution.py:73
  39.9 295.0 %all-gather.2.cloned.1.call-start = ((), (), s32[]{:S(2)}) async-start(), calls=%async_computation.7 | async-start | bytes 1114112 | tf_op jit(solution)/shard_map/all_gather | solution.py:134
  208.2 4.6 %copy-start.5 = (s32[16]{0:T(128)S(1)}, s32[16]{0:T(128)}, u32[]{:S(2)}) copy-start(s32[16]{0:T(128)} %param.22) | copy-start | bytes 196
  212.3 206.7 %reduce-scatter.11.cloned.1.call-start = ((), (), s32[]{:S(2)}) async-start(), calls=%async_computation.8 | async-start | bytes 1114112 | tf_op jit(solution)/shard_map/reduce_scatter | solution.py:149
  337.9 17.2 %copy-start.2 = (bf16[8,1,128,128]{3,2,1,0:T(8,128)(2,1)S(1)}, bf16[8,1,128,128]{3,2,1,0:T(8,128)(2,1)}, u32[]{:S(2)}) copy-start(bf16[8,1,128,128]{3,2,1,0:T(8,128)(2,1)} %param.18) | copy-start | bytes 786436
Sparse Core Ops, SparseCore 0:
  34.1 78.0 reduce-scatter.8
  115.8 90.2 reduce-scatter.6
  209.5 76.2 reduce-scatter.4
  288.1 46.8 all-gather.1
  361.0 58.0 reduce-scatter.10
where the time goes:
time: 428 us; the launch traced here: 427 us
  waiting for transfers between devices  282 us (66%)
  blocking collectives  78.7 us (18%)
  matrix products  33.9 us (8%)
  between operations  15.4 us (4%)
  local copies, waits for them, and re-layouts  10.6 us (2%)
  other arithmetic  6.49 us (2%)
    reduce_scatter x1, waiting for transfers between devices, per_device(): lax.psum_scatter(query_part, 'gx', scatter_dimension=0, tiled=True)  92.9 us
    reduce_scatter x1, waiting for transfers between devices, per_device(): lax.psum_scatter(router_part, 'gx', scatter_dimension=0, tiled=True)  72.9 us
    reduce_scatter x1, waiting for transfers between devices, per_device(): lax.psum_scatter(jnp.einsum('tehd,ehdo->to', folded, wide_output, precisi...  58.2 us
    unnamed x1, blocking collectives  37.2 us
    reduce_scatter x1, waiting for transfers between devices, per_device(): lax.psum_scatter(keyval_part, 'gx', scatter_dimension=0, tiled=True)  30 us
    all_gather x1, waiting for transfers between devices, per_device(): lax.all_gather(attended_output, 'gx', axis=0, tiled=True)  27.6 us
    all_gather x1, blocking collectives, per_device(): gathered = lax.all_gather(tokens, 'gy', axis=0, tiled=True)  21.6 us
    all_gather x1, blocking collectives, per_device(): lax.all_gather(gate_weights, 'gx', axis=0, tiled=True)  19.8 us
  transfers between devices with their start and end apart: 5, of which 5 were waited for; matrix products, arithmetic and copies ran while one was open for 4% of the time, Pallas kernels for 0%

commit v1 on v0

--- a/solution.py
+++ b/solution.py
@@ -131,7 +131,9 @@
         attended_output.reshape(heads_local, new_len, top_count, head_dim), (1, 2, 0, 3)
     ).reshape(new_len, top_count * heads_local * head_dim)
     all_attended, all_gates = (
-        lax.all_gather(attended_output, "gx", axis=0, tiled=True),
+        jnp.concatenate(
+            lax.all_to_all(jnp.stack([attended_output] * lax.axis_size("gx")), "gx", 0, 0), axis=0
+        ),
         lax.all_gather(gate_weights, "gx", axis=0, tiled=True),
     )
     token_attended = jnp.take(

time: 428 us -> 406 us (0.949)
  waiting for transfers between devices: 282 us -> 246 us
  starting transfers between devices: 0.17 us -> 14.4 us
    all_gather x1 -> x0, waiting for transfers between devices: 27.6 us -> none  [per_device(): lax.all_gather(attended_output, 'gx', axis=0, tiled=True)]
    all_to_all x0 -> x1, starting transfers between devices: none -> 14.3 us  [per_device(): lax.all_to_all(jnp.stack([attended_output] * lax.axis_size('gx')), 'gx',...]
    reduce_scatter x1, waiting for transfers between devices: 72.9 us -> 64.1 us  [per_device(): lax.psum_scatter(router_part, 'gx', scatter_dimension=0, tiled=True)]
  transfers between devices with their start and end apart: 5 -> 5, of which waited for: 5 -> 4; matrix products, arithmetic and copies ran while one was open for 4% -> 5% of each run, Pallas kernels for 0% -> 0%
where the time goes in v1:
time: 406 us; the launch traced here: 405 us
  waiting for transfers between devices  246 us (61%)
  blocking collectives  78.4 us (19%)
  matrix products  34 us (8%)
  between operations  15.4 us (4%)
  starting transfers between devices  14.4 us (4%)
  local copies, waits for them, and re-layouts  10.3 us (3%)
  other arithmetic  6.51 us (2%)
    reduce_scatter x1, waiting for transfers between devices, per_device(): lax.psum_scatter(query_part, 'gx', scatter_dimension=0, tiled=True)  93.3 us
    reduce_scatter x1, waiting for transfers between devices, per_device(): lax.psum_scatter(router_part, 'gx', scatter_dimension=0, tiled=True)  64.1 us
    reduce_scatter x1, waiting for transfers between devices, per_device(): lax.psum_scatter(jnp.einsum('tehd,ehdo->to', folded, wide_output, precisi...  58.7 us
    unnamed x1, blocking collectives  37.1 us
    reduce_scatter x1, waiting for transfers between devices, per_device(): lax.psum_scatter(keyval_part, 'gx', scatter_dimension=0, tiled=True)  29.5 us
    all_gather x1, blocking collectives, per_device(): gathered = lax.all_gather(tokens, 'gy', axis=0, tiled=True)  21.6 us
    all_gather x1, blocking collectives, per_device(): lax.all_gather(gate_weights, 'gx', axis=0, tiled=True)  19.6 us
    dot_general x1, matrix products, per_device(): jnp.einsum('tse,tshd->tehd', mixing, piece, precision=lax.Precision.HIGHEST)  17.3 us
  transfers between devices with their start and end apart: 5, of which 4 were waited for; matrix products, arithmetic and copies ran while one was open for 5% of the time, Pallas kernels for 0%

profile of v1, /device:TPU:8, one launch (start us, length us, event | category | flops | bytes accessed | tf_op | source)
XLA Modules:
  0.0 404.7 jit_solution(5366508733099869309)
XLA Ops:
  6.5 0.7 compare_select_fusion.3
  7.2 0.6 scatter_custom_fusion
  7.9 0.7 convert_element_type.98
  8.6 21.6 %all_gather.6 = bf16[2048,128]{1,0:T(8,128)(2,1)S(1)} all-gather(bf16[128,128]{1,0:T(8,128)(2,1)} %param.13), channel_id=1, replica_groups=mesh['gx'=16,'gy'=16] {'gy'}, dimensions={0}, use_global_device_ids=true | all-gather | bytes 557056 | tf_op jit(solution)/shard_map/all_gather | solution.py:46
  30.2 0.6 gather_fusion.1
  30.9 0.4 fusion.24
  31.3 2.7 convolution_bitcast_fusion.2
  33.9 0.0 reduce-scatter.9.cloned.1.call-update
  34.0 0.0 reduce-scatter.7.cloned.1.call-start
  34.0 0.0 copy-done
  34.0 0.0 copy-start.3
  34.0 0.0 copy-start.4
  34.1 0.0 copy-start.5
  34.1 0.0 copy-start.1
  34.1 4.5 %convolution_bitcast_fusion.1 = f32[2048,8,1,128]{3,0,1,2:T(8,128)} fusion(bf16[2048,128,1]{1,0,2:T(8,128)(2,1)S(1)} %bitcast.114, bf16[8,128,1,128]{3,1,2,0:T(8,128)(2,1)S(1)} %copy-done), kind=kOutput, calls=%fused_computation.25 | convolution fusion | flops 536870912 | bytes 9175040 | tf_op jit(solution)/shard_map/td,edhk->tehk/dot_general | solution.py:62
  38.5 0.0 reduce-scatter.7.cloned.1.call-update
  38.6 0.0 reduce-scatter.5.cloned.1.call-start
  38.6 0.1 broadcast_bitcast_fusion
  38.7 0.4 bitcast_select_fusion
  39.1 0.9 fusion.29
  39.9 0.0 reduce-scatter.5.cloned.1.call-update
  40.0 0.6 dynamic-slice.4
  41.3 0.0 copy-done.5
  41.3 0.6 dynamic-slice.5
  42.5 0.1 broadcast_bitcast_fusion.1
  42.6 0.1 dynamic-slice.8
  42.7 0.4 copy.41
  43.1 0.6 gather_fusion
  43.7 0.1 copy.43
  43.8 37.1 %all-reduce = f32[2048]{0:T(1024)S(1)} all-reduce(f32[2048]{0:T(1024)S(1)} %bitcast.126), channel_id=3, replica_groups=mesh['gx'=16,'gy'=16] {'gx'}, use_global_device_ids=true, to_apply=%region_3.4.clone | all-reduce | flops 2048 | bytes 16384
  81.0 0.6 dynamic-slice.6
  82.2 0.1 fusion.44
  82.3 0.1 mul.177
  82.4 0.2 mul.178
  82.5 29.5 %reduce-scatter.9.cloned.1.call-done = f32[128,1,256]{2,0,1:T(8,128)} async-done(((f32[2048,1,256]{2,0,1:T(8,128)}), f32[128,1,256]{2,0,1:T(8,128)}) %reduce-scatter.9.cloned.1.call-update) | async-done | bytes 131088 | tf_op jit(solution)/shard_map/reduce_scatter | solution.py:72
  112.1 1.0 fusion.38
  113.1 93.3 %reduce-scatter.7.cloned.1.call-done = f32[128,8,1,128]{3,0,1,2:T(8,128)} async-done(((f32[2048,8,1,128]{3,0,1,2:T(8,128)}), f32[128,8,1,128]{3,0,1,2:T(8,128)}) %reduce-scatter.7.cloned.1.call-update) | async-done | bytes 524304 | tf_op jit(solution)/shard_map/reduce_scatter | solution.py:71
  206.4 1.3 copy.44
  207.7 0.4 multiply_reduce_fusion
  208.1 0.2 multiply_convert_fusion.3
  208.3 0.1 fusion.34
  208.5 3.0 while.16
  208.5 1.3 fusion.62
  209.9 0.2 fusion.63
  210.1 1.3 fusion.64
  211.5 0.2 fusion.50
  211.7 0.2 fusion.23
  212.0 1.1 stack.10
  213.1 14.3 %all-to-all-start = ((bf16[16,128,256]{2,1,0:T(8,128)(2,1)}), bf16[16,128,256]{2,1,0:T(8,128)(2,1)S(1)}, u32[]{:S(2)}, u32[]{:S(2)}) async-start(bf16[16,128,256]{2,1,0:T(8,128)(2,1)} %stack.10), calls=%async_computation.3 | async-start | bytes 2097152 | tf_op jit(solution)/shard_map/all_to_all | solution.py:135
  227.4 0.0 reduce-scatter.11.cloned.1.call-start
  227.4 64.1 %reduce-scatter.5.cloned.1.call-done = f32[128,8]{0,1:T(8,128)} async-done(((f32[2048,8]{0,1:T(8,128)}), f32[128,8]{0,1:T(8,128)}) %reduce-scatter.5.cloned.1.call-update) | async-done | bytes 4112 | tf_op jit(solution)/shard_map/reduce_scatter | solution.py:73
  291.5 0.7 broadcast_multiply_fusion
  292.3 19.6 %all_gather.7 = bf16[2048,2]{0,1:T(2,128)(2,1)S(1)} all-gather(bf16[128,2]{0,1:T(2,128)(2,1)S(1)} %pad_maximum_fusion), channel_id=1, replica_groups=mesh['gx'=16,'gy'=16] {'gx'}, dimensions={0}, use_global_device_ids=true | all-gather | bytes 8704 | tf_op jit(solution)/shard_map/all_gather | solution.py:137
  311.9 0.6 gather_fusion.2
  312.5 1.4 copy.42
  313.9 0.0 all-to-all-done
  313.9 0.6 gather_fusion.3
  314.6 0.5 gather.40
  315.0 0.0 copy-start.2
  315.1 17.3 %fusion.18 = f32[2048,8,128]{2,1,0:T(8,128)S(1)} fusion(bf16[2048,2,128]{2,1,0:T(2,128)(2,1)S(1)} %gather.40, pred[2048]{0:T(1024)(128)(4,1)S(1)} %broadcast_bitcast_fusion.1, f32[2048,2]{1,0:T(8,128)} %copy.42, s32[2048,2]{1,0:T(8,128)S(1)} %copy.41), kind=kOutput, calls=%fused_computation.29 | convolution fusion | flops 50921472 | bytes 9472000 | tf_op jit(solution)/shard_map/tse,tshd->tehd/dot_general | solution.py:150
  332.3 5.6 %fusion.15 = f32[2048,128]{1,0:T(8,128)} fusion(f32[2048,8,128]{2,1,0:T(8,128)S(1)} %fusion.18, bf16[8,1,128,128]{3,2,1,0:T(8,128)(2,1)S(1)} %copy-done.2), kind=kOutput, calls=%fused_computation.28 | convolution fusion | flops 3221225472 | bytes 9699328 | tf_op jit(solution)/shard_map/tehd,ehdo->to/dot_general | solution.py:152
  338.0 0.0 reduce-scatter.11.cloned.1.call-update
  338.0 58.7 %reduce-scatter.11.cloned.1.call-done = f32[128,128]{1,0:T(8,128)} async-done(((f32[2048,128]{1,0:T(8,128)}), f32[128,128]{1,0:T(8,128)}) %reduce-scatter.11.cloned.1.call-update) | async-done | bytes 65552 | tf_op jit(solution)/shard_map/reduce_scatter | solution.py:151
  396.7 1.5 convert_element_type.111
  (32 shorter events, 0.3 us)
Async XLA Ops:
  6.5 27.5 %copy-start = (bf16[8,128,1,128]{3,1,2,0:T(8,128)(2,1)S(1)}, bf16[8,128,1,128]{3,1,2,0:T(8,128)(2,1)}, u32[]{:S(2)}) copy-start(bf16[8,128,1,128]{3,1,2,0:T(8,128)(2,1)} %param.16) | copy-start | bytes 786436
  6.5 105.5 %reduce-scatter.9.cloned.1.call-start = ((), (), s32[]{:S(2)}) async-start(), calls=%async_computation.7 | async-start | bytes 2228224 | tf_op jit(solution)/shard_map/reduce_scatter | solution.py:72
  34.0 172.4 %reduce-scatter.7.cloned.1.call-start = ((), (), s32[]{:S(2)}) async-start(), calls=%async_computation.6 | async-start | bytes 8912896 | tf_op jit(solution)/shard_map/reduce_scatter | solution.py:71
  34.0 5.0 %copy-start.3 = (bf16[128,8]{0,1:T(8,128)(2,1)S(1)}, bf16[128,8]{0,1:T(8,128)(2,1)}, u32[]{:S(2)}) copy-start(bf16[128,8]{0,1:T(8,128)(2,1)} %param.15) | copy-start | bytes 6148
  34.0 5.9 %copy-start.4 = (s32[16]{0:T(128)S(1)}, s32[16]{0:T(128)}, u32[]{:S(2)}) copy-start(s32[16]{0:T(128)} %param.22) | copy-start | bytes 196
  34.1 7.2 %copy-start.5 = (s32[16]{0:T(128)S(1)}, s32[16]{0:T(128)}, u32[]{:S(2)}) copy-start(s32[16]{0:T(128)} %param.21) | copy-start | bytes 196
  34.1 8.6 %copy-start.1 = (s32[2048,2]{0,1:T(2,128)S(1)}, s32[2048,2]{0,1:T(2,128)}, u32[]{:S(2)}) copy-start(s32[2048,2]{0,1:T(2,128)} %param.23) | copy-start | bytes 49156
  38.5 42.4 %copy-start.6 = (u32[256]{0:T(256)S(1)}, u32[256]{0:T(256)}, u32[]{:S(2)}) copy-start(u32[256]{0:T(256)} %constant.201) | copy-start | bytes 3076
  38.6 253.0 %reduce-scatter.5.cloned.1.call-start = ((), (), s32[]{:S(2)}) async-start(), calls=%async_computation.5 | async-start | bytes 69632 | tf_op jit(solution)/shard_map/reduce_scatter | solution.py:73
  213.1 100.9 %all-to-all-start = ((bf16[16,128,256]{2,1,0:T(8,128)(2,1)}), bf16[16,128,256]{2,1,0:T(8,128)(2,1)S(1)}, u32[]{:S(2)}, u32[]{:S(2)}) async-start(bf16[16,128,256]{2,1,0:T(8,128)(2,1)} %stack.10), calls=%async_computation.3 | async-start | bytes 2097152 | tf_op jit(solution)/shard_map/all_to_all | solution.py:135
  227.4 169.3 %reduce-scatter.11.cloned.1.call-start = ((), (), s32[]{:S(2)}) async-start(), calls=%async_computation.8 | async-start | bytes 1114112 | tf_op jit(solution)/shard_map/reduce_scatter | solution.py:151
  315.0 17.3 %copy-start.2 = (bf16[8,1,128,128]{3,2,1,0:T(8,128)(2,1)S(1)}, bf16[8,1,128,128]{3,2,1,0:T(8,128)(2,1)}, u32[]{:S(2)}) copy-start(bf16[8,1,128,128]{3,2,1,0:T(8,128)(2,1)} %param.18) | copy-start | bytes 786436
Sparse Core Ops, SparseCore 0:
  34.1 77.9 reduce-scatter.8
  115.8 90.5 reduce-scatter.6
  209.8 81.6 reduce-scatter.4
  338.1 58.5 reduce-scatter.10
